TPU v7x, 128 devices: a whole 4x4x4 slice. The times are simulated.
128 devices in a mesh: gx: 8 (over y_hi, z), gy: 16 (over x, y_lo, core).
Axes of the slice: x: 4, y: 4 (y_hi: 2, y_lo: 2; y = y_hi * 2 + y_lo), z: 4, core: 2. Of those that a mesh axis runs over, the one named last changes fastest.
Arguments:
- observed: float32 [2, 8192, 8192], P(None, 'gx', 'gy'), may hold values from -6 to 6
- noise_var: float32 [8192, 8192], P('gx', 'gy'), may hold values from 0.05 to 0.5
- row_kernel: float32 [4096, 4096], P('gx'), may hold values from -1 to 1.2, as said below
- col_kernel: float32 [4096, 4096], P('gy'), may hold values from -1 to 1.2, as said below
Outputs:
- gram_times: float32 [2, 8192, 8192], P(None, 'gx', 'gy')
Inputs may be any that keep to these rules, and one draw needn't show every extreme that they name: row_kernel is symmetric. col_kernel is symmetric.
All inputs are finite; a program needn't handle non-finite values.
Results may differ from a plain program's by a relative error of at most 0.000065.
Values sent between devices are 32-bit elements; how exact they have to be, the bound alone decides.
No kernel may reach another device: no remote copies, remote signals or barrier semaphores. Data moves between devices by JAX's collectives and lax.ppermute only.
A program may use at most 128 MiB of HBM per device.

v0:
```python
import jax
import jax.numpy as jnp
from jax import lax
from jax.sharding import Mesh, PartitionSpec as P


def axis_count(axis):
    return lax.psum(1, axis)


def with_halo(cells, sides, width):
    for axis, dim in sides:
        count = axis_count(axis)
        ends = count - 1
        head = lax.slice_in_dim(cells, 0, width, axis=dim)
        tail = lax.slice_in_dim(cells, cells.shape[dim] - width, cells.shape[dim], axis=dim)
        cells = jnp.concatenate(
            [
                lax.ppermute(tail, axis, [(i, (i + 1) % count) for i in range(ends)]),
                cells,
                lax.ppermute(head, axis, [((i + 1) % count, i) for i in range(ends)]),
            ],
            axis=dim,
        )
    return cells


def edges(cells, axis, dim, width):
    count = axis_count(axis)
    ends = count - 1
    head = lax.slice_in_dim(cells, 0, width, axis=dim)
    tail = lax.slice_in_dim(cells, cells.shape[dim] - width, cells.shape[dim], axis=dim)
    before = lax.ppermute(tail, axis, [(i, i + 1) for i in range(ends)])
    after = lax.ppermute(head, axis, [(i + 1, i) for i in range(ends)])
    return (before, after)


def keys_weight(dist):
    span = jnp.abs(dist)
    inner = (1.5 * span - 2.5) * span * span + 1.0
    outer = ((-0.5 * span + 2.5) * span - 4.0) * span + 2.0
    return jnp.where(span < 1.0, inner, jnp.where(span < 2.0, outer, 0.0))


def tap_table(rows, cols, coarse_on_rows, pad):
    r = lax.broadcasted_iota(jnp.float32, (rows, cols), 0)
    c = lax.broadcasted_iota(jnp.float32, (rows, cols), 1)
    if coarse_on_rows:
        coarse, fine = (r, c)
    else:
        coarse, fine = (c, r)
    if pad == 4:
        dist = coarse - ((fine - 4.0) * 0.5 + 0.25)
    else:
        dist = coarse - 2.0 - (fine * 0.5 + 0.25)
    return keys_weight(dist).astype(jnp.bfloat16)


def split3(x):
    hi = lax.reduce_precision(x, exponent_bits=8, mantissa_bits=7)
    rest = x - hi
    mid = lax.reduce_precision(rest, exponent_bits=8, mantissa_bits=7)
    lo = rest - mid
    return (hi.astype(jnp.bfloat16), mid.astype(jnp.bfloat16), lo.astype(jnp.bfloat16))


def exact_dot(eq, x, table, data_first):
    ins, _ = eq.split("->")
    first, second = ins.split(",")
    if data_first:
        parts = jnp.concatenate(split3(x), axis=first.index(second[0]))
        return jnp.einsum(
            eq, parts, jnp.concatenate([table] * 3, axis=0), preferred_element_type=jnp.float32
        )
    parts = jnp.concatenate(split3(x), axis=second.index(first[1]))
    return jnp.einsum(
        eq, jnp.concatenate([table] * 3, axis=1), parts, preferred_element_type=jnp.float32
    )


def row_windows(kernel, order, block, width):
    padded = jnp.pad(kernel, ((0, width - kernel.shape[0]), (2, width - block - 2)))
    return jnp.concatenate([padded[:, block * w : block * w + width] for w in order], axis=1)


def body(observed, noise_var, row_kernel, col_kernel):
    highest = lax.Precision.HIGH
    rows_axis = ("yh", "z")
    cols_axis = ("x", "yl", "core")
    tile_rows = row_kernel.shape[0]
    tile_cols = col_kernel.shape[0]
    ext_rows = tile_rows + 8
    row_count = axis_count(rows_axis)
    swap = [(0, 1), (1, 0)]
    side = lax.axis_index("yl")
    span = 4 * tile_cols
    quarters = range(col_kernel.shape[1] // span)
    low = jnp.concatenate(
        [col_kernel[:, q * span : q * span + span // 2] for q in quarters], axis=1
    )
    high = jnp.concatenate(
        [col_kernel[:, q * span + span // 2 : (q + 1) * span] for q in quarters], axis=1
    )
    near_cols = jnp.where(side == 0, low, high)
    far_cols = jnp.where(side == 0, high, low)
    partner_cols = lax.ppermute(far_cols, "yl", swap)
    row_rows = with_halo(row_kernel, ((rows_axis, 0),), 2)
    halves_n = axis_count("yh")
    depth = axis_count("z")
    order = [h * depth + d for d in range(depth) for h in range(halves_n)]
    row_big = row_windows(row_rows, order, tile_rows, ext_rows)
    before, after = edges(observed, cols_axis, 2, 4)
    col_adj = tap_table(2 * tile_cols + 8, tile_cols, False, 4)
    row_adj = tap_table(ext_rows, 2 * tile_rows, True, 2)
    colsum = (
        exact_dot("rpq,qj->rpj", observed, col_adj[4:-4], True)
        + exact_dot("rpq,qj->rpj", before, col_adj[:4], True)
        + exact_dot("rpq,qj->rpj", after, col_adj[-4:], True)
    )
    inducing = exact_dot("ip,rpj->rij", colsum, row_adj, False)
    half = lax.all_gather(inducing, ("x", "core"), axis=2, tiled=True)
    near = jnp.einsum("rik,jk->rij", half, near_cols, precision=highest)
    for_partner = jnp.einsum("rik,jk->rij", half, partner_cols, precision=highest)
    mixed = near + lax.ppermute(for_partner, "yl", swap)
    product = jnp.einsum(
        "ik,rkj->rij",
        row_big,
        lax.all_gather(mixed, ("z", "yh"), axis=1, tiled=True),
        precision=highest,
    )
    coarse_ext = with_halo(product, ((cols_axis, 2),), 2)
    row_fwd = tap_table(2 * tile_rows, ext_rows, False, 2)
    col_fwd = tap_table(tile_cols + 4, 2 * tile_cols, True, 2)
    rowpass = exact_dot("pi,rij->rpj", coarse_ext, row_fwd, False)
    result = exact_dot("rpj,jq->rpq", rowpass, col_fwd, True)
    return result + noise_var[None] * observed


def solution(mesh):
    rows_n, cols_n = mesh.devices.shape
    z = min(4, rows_n)
    shape = (rows_n // z, z, cols_n // 4, 2, 2)
    fine = Mesh(mesh.devices.reshape(shape), ("yh", "z", "x", "yl", "core"))
    rows = ("yh", "z")
    cols = ("x", "yl", "core")
    return jax.shard_map(
        body,
        mesh=fine,
        in_specs=(P(None, rows, cols), P(rows, cols), P(rows, None), P(cols, None)),
        out_specs=P(None, rows, cols),
        check_vma=False,
    )
```

profile of v0, /device:TPU:9, one launch (start us, length us, event | category | flops | bytes accessed | tf_op | source)
XLA Modules:
  0.0 259.7 jit_solution(11175421567967225632)
XLA Ops:
  6.5 1.9 fusion.117
  8.8 3.6 %collective-permute-start = (f32[2,1024,4]{1,2,0:T(4,128)S(1)}, f32[2,1024,4]{1,2,0:T(4,128)S(1)}, u32[]{:S(2)}, u32[]{:S(2)}) collective-permute-start(f32[2,1024,4]{1,2,0:T(4,128)S(1)} %copy.16), channel_id=1, source_target_pairs={{0,1},{1,2},{2,3},{3,4},{4,5},{5,6},{6,7},{7,8},{8,9},{9,10},{10,1... | collective-permute-start | bytes 98312 | tf_op jit(solution)/shard_map/ppermute | solution.py:33
  12.7 1.9 collective-permute-start.1
  14.6 3.2 %reduce-precision_convert_fusion.1 = (bf16[2,1024,512]{2,1,0:T(8,128)(2,1)S(1)}, bf16[2,1024,512]{2,1,0:T(8,128)(2,1)S(1)}, bf16[2,1024,512]{2,1,0:T(8,128)(2,1)S(1)}) fusion(f32[2,1024,512]{2,1,0:T(8,128)} %param.4), kind=kLoop, calls=%fused_computation.18 | loop fusion | flops 7340032 | bytes 10485760 | tf_op jit(solution)/shard_map/convert_element_type | solution.py:64
  18.2 1.3 fusion.40
  20.6 2.3 reduce-precision_convert_fusion.5
  22.9 2.8 %fusion.59 = f32[2,520,256]{2,1,0:T(8,128)} fusion(bf16[520,1024]{1,0:T(8,128)(2,1)S(1)} %fusion.40, bf16[2,1024,256]{2,1,0:T(8,128)(2,1)S(1)} %get-tuple-element.35, bf16[2,1024,256]{2,1,0:T(8,128)(2,1)S(1)} %get-tuple-element.36, bf16[2,1024,256]{2,1,0:T(8,128)(2,1)S(1)} %get-tuple-element.34), kind=kOutput, calls=%fused_computation.87 | convolution fusion | flops 1654800384 | bytes 5275648 | tf_op jit(solution)/shard_map/ip,rpj->rij/dot_general | solution.py:76
  25.7 2.6 %fusion.116 = (f32[256,512]{1,0:T(8,128)S(1)}, f32[256,512]{1,0:T(8,128)S(1)}, f32[256,512]{1,0:T(8,128)S(1)}, f32[256,512]{1,0:T(8,128)S(1)}, f32[256,512]{1,0:...) fusion(f32[256,4096]{1,0:T(8,128)} %param.7), kind=kLoop, calls=%fused_computation.161 | loop fusion | bytes 8388608 | tf_op jit(solution)/shard_map/slice | solution.py:99
  28.7 0.5 copy-done.2
  29.7 46.2 %collective-permute-done.2 = f32[256,2048]{1,0:T(8,128)} collective-permute-done((f32[256,2048]{1,0:T(8,128)S(1)}, f32[256,2048]{1,0:T(8,128)}, u32[]{:S(2)}, u32[]{:S(2)}) %collective-permute-start.2) | collective-permute-done | bytes 2097184 | tf_op jit(solution)/shard_map/ppermute | solution.py:106
  75.9 3.9 %all-gather.3.cloned.1.call-done = f32[2,520,2048]{2,1,0:T(8,128)} async-done(((f32[2,520,256]{2,1,0:T(8,128)}), f32[2,520,2048]{2,1,0:T(8,128)}) %all-gather.3.cloned.1.call-update) | async-done | bytes 8519696 | tf_op jit(solution)/shard_map/all_gather | solution.py:121
  79.8 6.9 %fusion.49 = f32[2,520,256]{2,1,0:T(8,128)S(1)} fusion(f32[2,520,2048]{2,1,0:T(8,128)} %all-gather.3.cloned.1.call-done, f32[256,2048]{1,0:T(8,128)} %collective-permute-done.2), kind=kOutput, calls=%fused_computation.79 | convolution fusion | flops 3271557120 | bytes 11681792 | tf_op jit(solution)/shard_map/rik,jk->rij/dot_general | solution.py:123
  87.2 3.5 %fusion.51 = f32[2,520,256]{2,1,0:T(8,128)S(1)} fusion(f32[2,520,2048]{2,1,0:T(8,128)S(1)} %copy-done, f32[256,512]{1,0:T(8,128)S(1)} %copy-done.3, f32[256,512]{1,0:T(8,128)S(1)} %copy-done.5, f32[256,512]{1,0:T(8,128)S(1)} %get-tuple-element.16, f32[256,512]{1,0:T(8,128)S(1)} %get-tuple-element.17, f32[256,512]{1,0:T(8,128)S(1)} %get-tuple-element.18, ...), kind=kOutput, calls=%fused_computation.81 | convolution fusion | flops 3275227136 | bytes 13778945 | tf_op jit(solution)/shard_map/rik,jk->rij/dot_general | solution.py:122
  90.7 21.1 %collective-permute-done.3 = f32[2,520,256]{2,1,0:T(8,128)S(1)} collective-permute-done((f32[2,520,256]{2,1,0:T(8,128)S(1)}, f32[2,520,256]{2,1,0:T(8,128)S(1)}, u32[]{:S(2)}, u32[]{:S(2)}) %collective-permute-start.3) | collective-permute-done | bytes 1064992 | tf_op jit(solution)/shard_map/ppermute | solution.py:124
  111.8 1.1 add.216
  113.0 1.0 fusion.115
  114.0 3.2 %collective-permute-start.4 = (f32[2,4096]{1,0:T(2,128)S(1)}, f32[2,4096]{1,0:T(2,128)S(1)}, u32[]{:S(2)}, u32[]{:S(2)}) collective-permute-start(f32[2,4096]{1,0:T(2,128)S(1)} %get-tuple-element.13), channel_id=1, source_target_pairs={{0,16},{16,32},{32,48},{48,64},{64,80},{80,96},{96,112},{1,17},{17... | collective-permute-start | bytes 98312 | tf_op jit(solution)/shard_map/ppermute | solution.py:19
  117.2 1.3 collective-permute-start.5
  118.5 2.3 fusion.43
  120.7 1.1 collective-permute-done.5
  121.8 10.9 %select_maximum_fusion = f32[520,4104]{1,0:T(8,128)S(1)} fusion(f32[2,4096]{1,0:T(2,128)S(1)} %collective-permute-done.5, f32[512,4096]{1,0:T(8,128)} %param.6, f32[2,4096]{1,0:T(2,128)S(1)} %collective-permute-done.4), kind=kLoop, calls=%fused_computation.2 | loop fusion | flops 27743040 | bytes 16990464 | tf_op jit(solution)/shard_map/concatenate | solution.py:17
  132.7 3.4 %fusion.114 = (f32[520,520]{1,0:T(8,128)S(1)}, f32[520,520]{1,0:T(8,128)S(1)}, f32[520,520]{1,0:T(8,128)}, f32[520,520]{1,0:T(8,128)}, f32[520,520]{1,0:T(8,128)...) fusion(f32[520,4104]{1,0:T(8,128)S(1)} %select_maximum_fusion), kind=kLoop, calls=%fused_computation.159 | loop fusion | bytes 17305600 | tf_op jit(solution)/shard_map/slice | solution.py:83
  136.1 11.6 %concatenate.62 = f32[520,4160]{1,0:T(8,128)} concatenate(f32[520,520]{1,0:T(8,128)} %get-tuple-element.12, f32[520,520]{1,0:T(8,128)} %get-tuple-element.11, f32[520,520]{1,0:T(8,128)} %get-tuple-element.10, f32[520,520]{1,0:T(8,128)} %get-tuple-element.9, f32[520,520]{1,0:T(8,128)} %get-tuple-element.8, f32[520,520]{1,0:T(8,128)} %get-tuple-element.7, ...), dimensions={1} | concatenate | bytes 17305600 | tf_op jit(solution)/shard_map/concatenate | solution.py:83
  147.7 73.1 %all-gather.5.cloned.1.call-done = f32[2,4160,256]{2,1,0:T(8,128)} async-done(((f32[2,520,256]{2,1,0:T(8,128)}), f32[2,4160,256]{2,1,0:T(8,128)}) %all-gather.5.cloned.1.call-update) | async-done | bytes 8519696 | tf_op jit(solution)/shard_map/all_gather | solution.py:128
  220.9 12.2 %fusion.62 = f32[2,520,256]{2,1,0:T(8,128)S(1)} fusion(f32[2,4160,256]{2,1,0:T(8,128)} %all-gather.5.cloned.1.call-done, f32[520,4160]{1,0:T(8,128)} %concatenate.62), kind=kOutput, calls=%fused_computation.88 | convolution fusion | flops 6645350400 | bytes 18237440 | tf_op jit(solution)/shard_map/ik,rkj->rij/dot_general | solution.py:125
  233.5 4.9 %collective-permute-start.6 = (f32[2,520,2]{1,2,0:T(2,128)S(1)}, f32[2,520,2]{1,2,0:T(2,128)S(1)}, u32[]{:S(2)}, u32[]{:S(2)}) collective-permute-start(f32[2,520,2]{1,2,0:T(2,128)S(1)} %copy.10), channel_id=1, source_target_pairs={{0,1},{1,2},{2,3},{3,4},{4,5},{5,6},{6,7},{7,8},{8,9},{9,10},{10,1... | collective-permute-start | bytes 24968 | tf_op jit(solution)/shard_map/ppermute | solution.py:19
  238.7 2.1 collective-permute-start.7
  241.4 3.1 %collective-permute-done.7 = f32[2,520,2]{1,2,0:T(2,128)S(1)} collective-permute-done((f32[2,520,2]{1,2,0:T(2,128)S(1)}, f32[2,520,2]{1,2,0:T(2,128)S(1)}, u32[]{:S(2)}, u32[]{:S(2)}) %collective-permute-start.7) | collective-permute-done | bytes 8352 | tf_op jit(solution)/shard_map/ppermute | solution.py:21
  244.8 0.7 reduce-precision_convert_fusion.7
  245.5 0.5 copy-done.6
  246.0 2.5 reduce-precision_convert_fusion.3
  248.9 4.0 %multiply_add_fusion = f32[2,1024,512]{2,1,0:T(8,128)} fusion(f32[2,1024,512]{2,1,0:T(8,128)S(1)} %copy-done.1, f32[1024,512]{1,0:T(8,128)S(1)} %copy-done.7, bf16[2,1024,260]{1,2,0:T(8,128)(2,1)S(1)} %get-tuple-element.29, bf16[2,1024,260]{1,2,0:T(8,128)(2,1)S(1)} %get-tuple-element.30, bf16[2,1024,260]{1,2,0:T(8,128)(2,1)S(1)} %get-tuple-element.28, ...), kind=kOutput, calls=%fused_computation.20 | convolution fusion | flops 1649856512 | bytes 13946880 | tf_op jit(solution)/shard_map/rpj,jq->rpq/dot_general | solution.py:72
  (45 shorter events, 5.3 us)
Async XLA Ops:
  6.5 73.2 %all-gather.3.cloned.1.call-start = ((), (), s32[]{:S(2)}) async-start(), calls=%async_computation | async-start | bytes 9584640 | tf_op jit(solution)/shard_map/all_gather | solution.py:121
  8.8 10.8 %collective-permute-start = (f32[2,1024,4]{1,2,0:T(4,128)S(1)}, f32[2,1024,4]{1,2,0:T(4,128)S(1)}, u32[]{:S(2)}, u32[]{:S(2)}) collective-permute-start(f32[2,1024,4]{1,2,0:T(4,128)S(1)} %copy.16), channel_id=1, source_target_pairs={{0,1},{1,2},{2,3},{3,4},{4,5},{5,6},{6,7},{7,8},{8,9},{9,10},{10,1... | collective-permute-start | bytes 98312 | tf_op jit(solution)/shard_map/ppermute | solution.py:33
  12.7 7.4 %collective-permute-start.1 = (f32[2,1024,4]{1,2,0:T(4,128)S(1)}, f32[2,1024,4]{1,2,0:T(4,128)S(1)}, u32[]{:S(2)}, u32[]{:S(2)}) collective-permute-start(f32[2,1024,4]{1,2,0:T(4,128)S(1)} %copy.17), channel_id=1, source_target_pairs={{1,0},{2,1},{3,2},{4,3},{5,4},{6,5},{7,6},{8,7},{9,8},{10,9},{11,1... | collective-permute-start | bytes 98312 | tf_op jit(solution)/shard_map/ppermute | solution.py:34
  25.7 195.2 %all-gather.5.cloned.1.call-start = ((), (), s32[]{:S(2)}) async-start(), calls=%async_computation.1 | async-start | bytes 9584640 | tf_op jit(solution)/shard_map/all_gather | solution.py:128
  28.4 0.8 copy-start.2
  28.4 1.0 copy-start.4
  29.3 46.5 %collective-permute-start.2 = (f32[256,2048]{1,0:T(8,128)S(1)}, f32[256,2048]{1,0:T(8,128)}, u32[]{:S(2)}, u32[]{:S(2)}) collective-permute-start(f32[256,2048]{1,0:T(8,128)S(1)} %fusion.65), channel_id=1, source_target_pairs={{0,2},{2,0},{1,3},{3,1},{4,6},{6,4},{5,7},{7,5},{8,10},{10,8},{9,1... | collective-permute-start | bytes 6291464 | tf_op jit(solution)/shard_map/ppermute | solution.py:106
  79.8 7.4 %copy-start = (f32[2,520,2048]{2,1,0:T(8,128)S(1)}, f32[2,520,2048]{2,1,0:T(8,128)}, u32[]{:S(2)}) copy-start(f32[2,520,2048]{2,1,0:T(8,128)} %all-gather.3.cloned.1.call-done) | copy-start | bytes 25559044
  79.8 7.4 %copy-start.3 = (f32[256,512]{1,0:T(8,128)S(1)}, f32[256,512]{1,0:T(8,128)}, u32[]{:S(2)}) copy-start(f32[256,512]{1,0:T(8,128)} %copy-done.2) | copy-start | bytes 1572868
  79.8 7.4 %copy-start.5 = (f32[256,512]{1,0:T(8,128)S(1)}, f32[256,512]{1,0:T(8,128)}, u32[]{:S(2)}) copy-start(f32[256,512]{1,0:T(8,128)} %copy-done.4) | copy-start | bytes 1572868
  86.7 25.1 %collective-permute-start.3 = (f32[2,520,256]{2,1,0:T(8,128)S(1)}, f32[2,520,256]{2,1,0:T(8,128)S(1)}, u32[]{:S(2)}, u32[]{:S(2)}) collective-permute-start(f32[2,520,256]{2,1,0:T(8,128)S(1)} %fusion.49), channel_id=1, source_target_pairs={{0,2},{2,0},{1,3},{3,1},{4,6},{6,4},{5,7},{7,5},{8,10},{10,8},{9,1... | collective-permute-start | bytes 3194888 | tf_op jit(solution)/shard_map/ppermute | solution.py:124
  114.0 6.8 %collective-permute-start.4 = (f32[2,4096]{1,0:T(2,128)S(1)}, f32[2,4096]{1,0:T(2,128)S(1)}, u32[]{:S(2)}, u32[]{:S(2)}) collective-permute-start(f32[2,4096]{1,0:T(2,128)S(1)} %get-tuple-element.13), channel_id=1, source_target_pairs={{0,16},{16,32},{32,48},{48,64},{64,80},{80,96},{96,112},{1,17},{17... | collective-permute-start | bytes 98312 | tf_op jit(solution)/shard_map/ppermute | solution.py:19
  117.2 4.7 %collective-permute-start.5 = (f32[2,4096]{1,0:T(2,128)S(1)}, f32[2,4096]{1,0:T(2,128)S(1)}, u32[]{:S(2)}, u32[]{:S(2)}) collective-permute-start(f32[2,4096]{1,0:T(2,128)S(1)} %get-tuple-element.14), channel_id=1, source_target_pairs={{16,0},{32,16},{48,32},{64,48},{80,64},{96,80},{112,96},{17,1},{33... | collective-permute-start | bytes 98312 | tf_op jit(solution)/shard_map/ppermute | solution.py:21
  233.5 7.7 %collective-permute-start.6 = (f32[2,520,2]{1,2,0:T(2,128)S(1)}, f32[2,520,2]{1,2,0:T(2,128)S(1)}, u32[]{:S(2)}, u32[]{:S(2)}) collective-permute-start(f32[2,520,2]{1,2,0:T(2,128)S(1)} %copy.10), channel_id=1, source_target_pairs={{0,1},{1,2},{2,3},{3,4},{4,5},{5,6},{6,7},{7,8},{8,9},{9,10},{10,1... | collective-permute-start | bytes 24968 | tf_op jit(solution)/shard_map/ppermute | solution.py:19
  238.7 5.9 %collective-permute-start.7 = (f32[2,520,2]{1,2,0:T(2,128)S(1)}, f32[2,520,2]{1,2,0:T(2,128)S(1)}, u32[]{:S(2)}, u32[]{:S(2)}) collective-permute-start(f32[2,520,2]{1,2,0:T(2,128)S(1)} %copy.11), channel_id=1, source_target_pairs={{1,0},{2,1},{3,2},{4,3},{5,4},{6,5},{7,6},{8,7},{9,8},{10,9},{11,1... | collective-permute-start | bytes 24968 | tf_op jit(solution)/shard_map/ppermute | solution.py:21
  244.8 1.2 copy-start.6
  246.0 2.5 copy-start.1
  246.0 2.9 %copy-start.7 = (f32[1024,512]{1,0:T(8,128)S(1)}, f32[1024,512]{1,0:T(8,128)}, u32[]{:S(2)}) copy-start(f32[1024,512]{1,0:T(8,128)} %param.5) | copy-start | bytes 6291460
Sparse Core Ops, SparseCore 0:
  25.8 53.9 all-gather.2
  113.1 107.7 all-gather.4
where the time goes:
time: 260 us
  waiting for transfers between devices  149 us (57%)
  matrix products  35.2 us (14%)
  local copies, waits for them, and re-layouts  23.9 us (9%)
  other arithmetic  20.5 us (8%)
  starting transfers between devices  17.9 us (7%)
  between operations  13.7 us (5%)
    all_gather x1, waiting for transfers between devices, body(): lax.all_gather(mixed, ('z', 'yh'), axis=1, tiled=True)  73.1 us
    ppermute x1, waiting for transfers between devices, body(): partner_cols = lax.ppermute(far_cols, 'yl', swap)  46.2 us
    ppermute x1, waiting for transfers between devices, body(): mixed = near + lax.ppermute(for_partner, 'yl', swap)  21.1 us
    dot_general x1, matrix products, body(): jnp.einsum('ik,rkj->rij', row_big, lax.all_gather(mixed, ('z', 'yh'), axi...  12.2 us
    concatenate x1, local copies, waits for them, and re-layouts, row_windows(): jnp.concatenate([padded[:, block * w:block * w + width] for w in order],...  11.6 us
    concatenate x1, other arithmetic, with_halo(): jnp.concatenate([lax.ppermute(tail, axis, [(i, (i + 1) % count) for i in...  10.9 us
    ppermute x2, starting transfers between devices, with_halo(): lax.ppermute(tail, axis, [(i, (i + 1) % count) for i in range(ends)])  8.12 us
    dot_general x4, matrix products, exact_dot(): jnp.einsum(eq, parts, jnp.concatenate([table] * 3, axis=0), preferred_ele...  7.22 us
  transfers between devices with their start and end apart: 10, of which 6 were waited for; matrix products, arithmetic and copies ran while one was open for 16% of the time, Pallas kernels for 0%

commit v1 on v0

--- a/solution.py
+++ b/solution.py
@@ -2,6 +2,11 @@
 import jax.numpy as jnp
 from jax import lax
 from jax.sharding import Mesh, PartitionSpec as P
+
+
+def exchange_gather(shard, name, dim):
+    repeated = jnp.stack([shard] * lax.axis_size(name))
+    return jnp.concatenate(lax.all_to_all(repeated, name, 0, 0), axis=dim)
 
 
 def axis_count(axis):
@@ -123,10 +128,7 @@
     for_partner = jnp.einsum("rik,jk->rij", half, partner_cols, precision=highest)
     mixed = near + lax.ppermute(for_partner, "yl", swap)
     product = jnp.einsum(
-        "ik,rkj->rij",
-        row_big,
-        lax.all_gather(mixed, ("z", "yh"), axis=1, tiled=True),
-        precision=highest,
+        "ik,rkj->rij", row_big, exchange_gather(mixed, ("z", "yh"), 1), precision=highest
     )
     coarse_ext = with_halo(product, ((cols_axis, 2),), 2)
     row_fwd = tap_table(2 * tile_rows, ext_rows, False, 2)

time: 260 us -> 283 us (1.088)
  waiting for transfers between devices: 149 us -> 160 us
  local copies, waits for them, and re-layouts: 23.9 us -> 33.9 us
  starting transfers between devices: 17.9 us -> 23.8 us
  matrix products: 35.2 us -> 30.6 us
    all_gather x1 -> x0, waiting for transfers between devices: 73.1 us -> none  [body(): lax.all_gather(mixed, ('z', 'yh'), axis=1, tiled=True)]
    ppermute x2, waiting for transfers between devices: 0.01 us -> 60.3 us  [with_halo(): lax.ppermute(tail, axis, [(i, (i + 1) % count) for i in range(ends)])]
    ppermute x2, waiting for transfers between devices: 4.19 us -> 28.2 us  [with_halo(): lax.ppermute(head, axis, [((i + 1) % count, i) for i in range(ends)])]
    all_to_all x0 -> x1, starting transfers between devices: none -> 5.7 us  [exchange_gather(): return jnp.concatenate(lax.all_to_all(repeated, name, 0, 0), axis=dim)]
    dot_general x1, matrix products: 12.2 us -> 7.59 us  [body(): jnp.einsum('ik,rkj->rij', row_big, exchange_gather(mixed, ('z', 'yh'), 1)...]
    reshape x0 -> x1, local copies, waits for them, and re-layouts: none -> 4.34 us  [exchange_gather(): return jnp.concatenate(lax.all_to_all(repeated, name, 0, 0), axis=dim)]
    another operation x0 -> x1, local copies, waits for them, and re-layouts: none -> 4.18 us  [exchange_gather(): repeated = jnp.stack([shard] * lax.axis_size(name))]
  transfers between devices with their start and end apart: 10 -> 10, of which waited for: 6 -> 6; matrix products, arithmetic and copies ran while one was open for 16% -> 15% of each run, Pallas kernels for 0% -> 0%
where the time goes in v1:
time: 283 us; the launch traced here: 281 us
  waiting for transfers between devices  160 us (57%)
  local copies, waits for them, and re-layouts  33.9 us (12%)
  matrix products  30.6 us (11%)
  starting transfers between devices  23.8 us (8%)
  other arithmetic  19.4 us (7%)
  between operations  13.7 us (5%)
    ppermute x2, waiting for transfers between devices, with_halo(): lax.ppermute(tail, axis, [(i, (i + 1) % count) for i in range(ends)])  60.3 us
    ppermute x1, waiting for transfers between devices, body(): partner_cols = lax.ppermute(far_cols, 'yl', swap)  46.2 us
    ppermute x2, waiting for transfers between devices, with_halo(): lax.ppermute(head, axis, [((i + 1) % count, i) for i in range(ends)])  28.2 us
    ppermute x1, waiting for transfers between devices, body(): mixed = near + lax.ppermute(for_partner, 'yl', swap)  21.1 us
    concatenate x1, local copies, waits for them, and re-layouts, row_windows(): jnp.concatenate([padded[:, block * w:block * w + width] for w in order],...  11.6 us
    concatenate x1, other arithmetic, with_halo(): jnp.concatenate([lax.ppermute(tail, axis, [(i, (i + 1) % count) for i in...  10.7 us
    ppermute x2, starting transfers between devices, with_halo(): lax.ppermute(tail, axis, [(i, (i + 1) % count) for i in range(ends)])  8.59 us
    dot_general x1, matrix products, body(): jnp.einsum('ik,rkj->rij', row_big, exchange_gather(mixed, ('z', 'yh'), 1)...  7.59 us
  transfers between devices with their start and end apart: 10, of which 6 were waited for; matrix products, arithmetic and copies ran while one was open for 15% of the time, Pallas kernels for 0%

profile of v1, /device:TPU:9, one launch (start us, length us, event | category | flops | bytes accessed | tf_op | source)
XLA Modules:
  0.0 281.2 jit_solution(1481416574945295032)
XLA Ops:
  6.5 1.9 fusion.117
  8.8 3.6 %collective-permute-start = (f32[2,1024,4]{1,2,0:T(4,128)S(1)}, f32[2,1024,4]{1,2,0:T(4,128)S(1)}, u32[]{:S(2)}, u32[]{:S(2)}) collective-permute-start(f32[2,1024,4]{1,2,0:T(4,128)S(1)} %copy.17), channel_id=1, source_target_pairs={{0,1},{1,2},{2,3},{3,4},{4,5},{5,6},{6,7},{7,8},{8,9},{9,10},{10,1... | collective-permute-start | bytes 98312 | tf_op jit(solution)/shard_map/ppermute | solution.py:38
  12.7 1.9 collective-permute-start.1
  14.6 3.2 %reduce-precision_convert_fusion.1 = (bf16[2,1024,512]{2,1,0:T(8,128)(2,1)S(1)}, bf16[2,1024,512]{2,1,0:T(8,128)(2,1)S(1)}, bf16[2,1024,512]{2,1,0:T(8,128)(2,1)S(1)}) fusion(f32[2,1024,512]{2,1,0:T(8,128)} %param.4), kind=kLoop, calls=%fused_computation.18 | loop fusion | flops 7340032 | bytes 10485760 | tf_op jit(solution)/shard_map/convert_element_type | solution.py:69
  18.2 1.3 fusion.40
  20.6 2.3 reduce-precision_convert_fusion.5
  22.9 2.8 fusion.59
  25.7 2.6 fusion.116
  29.7 46.2 %collective-permute-done.2 = f32[256,2048]{1,0:T(8,128)} collective-permute-done((f32[256,2048]{1,0:T(8,128)S(1)}, f32[256,2048]{1,0:T(8,128)}, u32[]{:S(2)}, u32[]{:S(2)}) %collective-permute-start.2) | collective-permute-done | bytes 2097184 | tf_op jit(solution)/shard_map/ppermute | solution.py:111
  75.8 4.0 %all-gather.2.cloned.1.call-done = f32[2,520,2048]{2,1,0:T(8,128)} async-done(((f32[2,520,256]{2,1,0:T(8,128)}), f32[2,520,2048]{2,1,0:T(8,128)}) %all-gather.2.cloned.1.call-update) | async-done | bytes 8519696 | tf_op jit(solution)/shard_map/all_gather | solution.py:126
  79.8 6.9 %fusion.49 = f32[2,520,256]{2,1,0:T(8,128)S(1)} fusion(f32[2,520,2048]{2,1,0:T(8,128)} %all-gather.2.cloned.1.call-done, f32[256,2048]{1,0:T(8,128)} %collective-permute-done.2), kind=kOutput, calls=%fused_computation.79 | convolution fusion | flops 3271557120 | bytes 11681792 | tf_op jit(solution)/shard_map/rik,jk->rij/dot_general | solution.py:128
  87.2 3.5 %fusion.51 = f32[2,520,256]{2,1,0:T(8,128)S(1)} fusion(f32[2,520,2048]{2,1,0:T(8,128)S(1)} %copy-done.1, f32[256,512]{1,0:T(8,128)S(1)} %copy-done.4, f32[256,512]{1,0:T(8,128)S(1)} %copy-done.6, f32[256,512]{1,0:T(8,128)S(1)} %get-tuple-element.16, f32[256,512]{1,0:T(8,128)S(1)} %get-tuple-element.17, f32[256,512]{1,0:T(8,128)S(1)} %get-tuple-element.18, ...), kind=kOutput, calls=%fused_computation.81 | convolution fusion | flops 3275227136 | bytes 13778945 | tf_op jit(solution)/shard_map/rik,jk->rij/dot_general | solution.py:127
  90.7 21.1 %collective-permute-done.3 = f32[2,520,256]{2,1,0:T(8,128)S(1)} collective-permute-done((f32[2,520,256]{2,1,0:T(8,128)S(1)}, f32[2,520,256]{2,1,0:T(8,128)S(1)}, u32[]{:S(2)}, u32[]{:S(2)}) %collective-permute-start.3) | collective-permute-done | bytes 1064992 | tf_op jit(solution)/shard_map/ppermute | solution.py:129
  112.0 4.2 %stack.2 = f32[8,2,520,256]{3,2,1,0:T(8,128)} broadcast(f32[2,520,256]{2,1,0:T(8,128)S(1)} %add.216), dimensions={1,2,3} | broadcast | bytes 9584640 | tf_op jit(solution)/shard_map/stack | solution.py:8
  116.2 5.7 %all-to-all-start = ((f32[8,2,520,256]{3,2,1,0:T(8,128)}), f32[8,2,520,256]{3,2,1,0:T(8,128)}, u32[]{:S(2)}, u32[]{:S(2)}) async-start(f32[8,2,520,256]{3,2,1,0:T(8,128)} %stack.2), calls=%async_computation | async-start | bytes 17039360 | tf_op jit(solution)/shard_map/all_to_all | solution.py:9
  121.8 1.0 fusion.115
  122.8 3.4 %collective-permute-start.4 = (f32[2,4096]{1,0:T(2,128)S(1)}, f32[2,4096]{1,0:T(2,128)S(1)}, u32[]{:S(2)}, u32[]{:S(2)}) collective-permute-start(f32[2,4096]{1,0:T(2,128)S(1)} %get-tuple-element.13), channel_id=1, source_target_pairs={{0,16},{16,32},{32,48},{48,64},{64,80},{80,96},{96,112},{1,17},{17... | collective-permute-start | bytes 98312 | tf_op jit(solution)/shard_map/ppermute | solution.py:24
  126.2 1.3 collective-permute-start.5
  127.5 2.3 fusion.43
  129.8 60.3 %collective-permute-done.4 = f32[2,4096]{1,0:T(2,128)S(1)} collective-permute-done((f32[2,4096]{1,0:T(2,128)S(1)}, f32[2,4096]{1,0:T(2,128)S(1)}, u32[]{:S(2)}, u32[]{:S(2)}) %collective-permute-start.4) | collective-permute-done | bytes 32800 | tf_op jit(solution)/shard_map/ppermute | solution.py:24
  190.1 24.8 %collective-permute-done.5 = f32[2,4096]{1,0:T(2,128)S(1)} collective-permute-done((f32[2,4096]{1,0:T(2,128)S(1)}, f32[2,4096]{1,0:T(2,128)S(1)}, u32[]{:S(2)}, u32[]{:S(2)}) %collective-permute-start.5) | collective-permute-done | bytes 32800 | tf_op jit(solution)/shard_map/ppermute | solution.py:26
  215.0 10.7 %select_maximum_fusion = f32[520,4104]{1,0:T(8,128)S(1)} fusion(f32[2,4096]{1,0:T(2,128)S(1)} %collective-permute-done.5, f32[512,4096]{1,0:T(8,128)} %param.6, f32[2,4096]{1,0:T(2,128)S(1)} %collective-permute-done.4), kind=kLoop, calls=%fused_computation.2 | loop fusion | flops 27743040 | bytes 16990464 | tf_op jit(solution)/shard_map/concatenate | solution.py:22
  225.7 3.3 %fusion.114 = (f32[520,520]{1,0:T(8,128)S(1)}, f32[520,520]{1,0:T(8,128)S(1)}, f32[520,520]{1,0:T(8,128)}, f32[520,520]{1,0:T(8,128)}, f32[520,520]{1,0:T(8,128)...) fusion(f32[520,4104]{1,0:T(8,128)S(1)} %select_maximum_fusion), kind=kLoop, calls=%fused_computation.159 | loop fusion | bytes 17305600 | tf_op jit(solution)/shard_map/slice | solution.py:88
  229.1 11.6 %concatenate.62 = f32[520,4160]{1,0:T(8,128)} concatenate(f32[520,520]{1,0:T(8,128)} %get-tuple-element.12, f32[520,520]{1,0:T(8,128)} %get-tuple-element.11, f32[520,520]{1,0:T(8,128)} %get-tuple-element.10, f32[520,520]{1,0:T(8,128)} %get-tuple-element.9, f32[520,520]{1,0:T(8,128)} %get-tuple-element.8, f32[520,520]{1,0:T(8,128)} %get-tuple-element.7, ...), dimensions={1} | concatenate | bytes 17305600 | tf_op jit(solution)/shard_map/concatenate | solution.py:88
  240.7 4.3 %copy.10 = f32[2,8,520,256]{3,2,1,0:T(8,128)S(1)} copy(f32[2,8,520,256]{3,2,0,1:T(8,128)} %bitcast.7) | data formatting | bytes 17039360 | tf_op jit(solution)/shard_map/reshape | solution.py:9
  245.1 1.6 copy-done
  246.6 7.6 %fusion.62 = f32[2,520,256]{2,1,0:T(8,128)S(1)} fusion(f32[2,4160,256]{2,1,0:T(8,128)S(1)} %bitcast.51, f32[520,4160]{1,0:T(8,128)S(1)} %copy-done), kind=kOutput, calls=%fused_computation.88 | convolution fusion | flops 6645350400 | bytes 18237440 | tf_op jit(solution)/shard_map/ik,rkj->rij/dot_general | solution.py:130
  254.6 5.2 %collective-permute-start.6 = (f32[2,520,2]{1,2,0:T(2,128)S(1)}, f32[2,520,2]{1,2,0:T(2,128)S(1)}, u32[]{:S(2)}, u32[]{:S(2)}) collective-permute-start(f32[2,520,2]{1,2,0:T(2,128)S(1)} %copy.11), channel_id=1, source_target_pairs={{0,1},{1,2},{2,3},{3,4},{4,5},{5,6},{6,7},{7,8},{8,9},{9,10},{10,1... | collective-permute-start | bytes 24968 | tf_op jit(solution)/shard_map/ppermute | solution.py:24
  260.1 1.9 collective-permute-start.7
  262.7 3.3 %collective-permute-done.7 = f32[2,520,2]{1,2,0:T(2,128)S(1)} collective-permute-done((f32[2,520,2]{1,2,0:T(2,128)S(1)}, f32[2,520,2]{1,2,0:T(2,128)S(1)}, u32[]{:S(2)}, u32[]{:S(2)}) %collective-permute-start.7) | collective-permute-done | bytes 8352 | tf_op jit(solution)/shard_map/ppermute | solution.py:26
  267.5 2.5 reduce-precision_convert_fusion.3
  270.3 4.0 %multiply_add_fusion = f32[2,1024,512]{2,1,0:T(8,128)} fusion(f32[2,1024,512]{2,1,0:T(8,128)S(1)} %copy-done.2, f32[1024,512]{1,0:T(8,128)S(1)} %copy-done.8, bf16[2,1024,260]{1,2,0:T(8,128)(2,1)S(1)} %get-tuple-element.29, bf16[2,1024,260]{1,2,0:T(8,128)(2,1)S(1)} %get-tuple-element.30, bf16[2,1024,260]{1,2,0:T(8,128)(2,1)S(1)} %get-tuple-element.28, ...), kind=kOutput, calls=%fused_computation.20 | convolution fusion | flops 1649856512 | bytes 13946880 | tf_op jit(solution)/shard_map/rpj,jq->rpq/dot_general | solution.py:77
  (48 shorter events, 7.2 us)
Async XLA Ops:
  6.5 73.2 %all-gather.2.cloned.1.call-start = ((), (), s32[]{:S(2)}) async-start(), calls=%async_computation.1 | async-start | bytes 9584640 | tf_op jit(solution)/shard_map/all_gather | solution.py:126
  8.8 10.8 %collective-permute-start = (f32[2,1024,4]{1,2,0:T(4,128)S(1)}, f32[2,1024,4]{1,2,0:T(4,128)S(1)}, u32[]{:S(2)}, u32[]{:S(2)}) collective-permute-start(f32[2,1024,4]{1,2,0:T(4,128)S(1)} %copy.17), channel_id=1, source_target_pairs={{0,1},{1,2},{2,3},{3,4},{4,5},{5,6},{6,7},{7,8},{8,9},{9,10},{10,1... | collective-permute-start | bytes 98312 | tf_op jit(solution)/shard_map/ppermute | solution.py:38
  12.7 7.4 %collective-permute-start.1 = (f32[2,1024,4]{1,2,0:T(4,128)S(1)}, f32[2,1024,4]{1,2,0:T(4,128)S(1)}, u32[]{:S(2)}, u32[]{:S(2)}) collective-permute-start(f32[2,1024,4]{1,2,0:T(4,128)S(1)} %copy.18), channel_id=1, source_target_pairs={{1,0},{2,1},{3,2},{4,3},{5,4},{6,5},{7,6},{8,7},{9,8},{10,9},{11,1... | collective-permute-start | bytes 98312 | tf_op jit(solution)/shard_map/ppermute | solution.py:39
  28.3 0.8 copy-start.3
  28.3 1.0 copy-start.5
  29.3 46.5 %collective-permute-start.2 = (f32[256,2048]{1,0:T(8,128)S(1)}, f32[256,2048]{1,0:T(8,128)}, u32[]{:S(2)}, u32[]{:S(2)}) collective-permute-start(f32[256,2048]{1,0:T(8,128)S(1)} %fusion.65), channel_id=1, source_target_pairs={{0,2},{2,0},{1,3},{3,1},{4,6},{6,4},{5,7},{7,5},{8,10},{10,8},{9,1... | collective-permute-start | bytes 6291464 | tf_op jit(solution)/shard_map/ppermute | solution.py:111
  79.8 7.4 %copy-start.1 = (f32[2,520,2048]{2,1,0:T(8,128)S(1)}, f32[2,520,2048]{2,1,0:T(8,128)}, u32[]{:S(2)}) copy-start(f32[2,520,2048]{2,1,0:T(8,128)} %all-gather.2.cloned.1.call-done) | copy-start | bytes 25559044
  79.8 7.4 %copy-start.4 = (f32[256,512]{1,0:T(8,128)S(1)}, f32[256,512]{1,0:T(8,128)}, u32[]{:S(2)}) copy-start(f32[256,512]{1,0:T(8,128)} %copy-done.3) | copy-start | bytes 1572868
  79.8 7.4 %copy-start.6 = (f32[256,512]{1,0:T(8,128)S(1)}, f32[256,512]{1,0:T(8,128)}, u32[]{:S(2)}) copy-start(f32[256,512]{1,0:T(8,128)} %copy-done.5) | copy-start | bytes 1572868
  86.7 25.1 %collective-permute-start.3 = (f32[2,520,256]{2,1,0:T(8,128)S(1)}, f32[2,520,256]{2,1,0:T(8,128)S(1)}, u32[]{:S(2)}, u32[]{:S(2)}) collective-permute-start(f32[2,520,256]{2,1,0:T(8,128)S(1)} %fusion.49), channel_id=1, source_target_pairs={{0,2},{2,0},{1,3},{3,1},{4,6},{6,4},{5,7},{7,5},{8,10},{10,8},{9,1... | collective-permute-start | bytes 3194888 | tf_op jit(solution)/shard_map/ppermute | solution.py:129
  116.2 124.5 %all-to-all-start = ((f32[8,2,520,256]{3,2,1,0:T(8,128)}), f32[8,2,520,256]{3,2,1,0:T(8,128)}, u32[]{:S(2)}, u32[]{:S(2)}) async-start(f32[8,2,520,256]{3,2,1,0:T(8,128)} %stack.2), calls=%async_computation | async-start | bytes 17039360 | tf_op jit(solution)/shard_map/all_to_all | solution.py:9
  122.8 67.3 %collective-permute-start.4 = (f32[2,4096]{1,0:T(2,128)S(1)}, f32[2,4096]{1,0:T(2,128)S(1)}, u32[]{:S(2)}, u32[]{:S(2)}) collective-permute-start(f32[2,4096]{1,0:T(2,128)S(1)} %get-tuple-element.13), channel_id=1, source_target_pairs={{0,16},{16,32},{32,48},{48,64},{64,80},{80,96},{96,112},{1,17},{17... | collective-permute-start | bytes 98312 | tf_op jit(solution)/shard_map/ppermute | solution.py:24
  126.2 88.8 %collective-permute-start.5 = (f32[2,4096]{1,0:T(2,128)S(1)}, f32[2,4096]{1,0:T(2,128)S(1)}, u32[]{:S(2)}, u32[]{:S(2)}) collective-permute-start(f32[2,4096]{1,0:T(2,128)S(1)} %get-tuple-element.14), channel_id=1, source_target_pairs={{16,0},{32,16},{48,32},{64,48},{80,64},{96,80},{112,96},{17,1},{33... | collective-permute-start | bytes 98312 | tf_op jit(solution)/shard_map/ppermute | solution.py:26
  240.7 5.9 %copy-start = (f32[520,4160]{1,0:T(8,128)S(1)}, f32[520,4160]{1,0:T(8,128)}, u32[]{:S(2)}) copy-start(f32[520,4160]{1,0:T(8,128)} %concatenate.62) | copy-start | bytes 25958404
  254.6 7.8 %collective-permute-start.6 = (f32[2,520,2]{1,2,0:T(2,128)S(1)}, f32[2,520,2]{1,2,0:T(2,128)S(1)}, u32[]{:S(2)}, u32[]{:S(2)}) collective-permute-start(f32[2,520,2]{1,2,0:T(2,128)S(1)} %copy.11), channel_id=1, source_target_pairs={{0,1},{1,2},{2,3},{3,4},{4,5},{5,6},{6,7},{7,8},{8,9},{9,10},{10,1... | collective-permute-start | bytes 24968 | tf_op jit(solution)/shard_map/ppermute | solution.py:24
  260.1 5.9 %collective-permute-start.7 = (f32[2,520,2]{1,2,0:T(2,128)S(1)}, f32[2,520,2]{1,2,0:T(2,128)S(1)}, u32[]{:S(2)}, u32[]{:S(2)}) collective-permute-start(f32[2,520,2]{1,2,0:T(2,128)S(1)} %copy.12), channel_id=1, source_target_pairs={{1,0},{2,1},{3,2},{4,3},{5,4},{6,5},{7,6},{8,7},{9,8},{10,9},{11,1... | collective-permute-start | bytes 24968 | tf_op jit(solution)/shard_map/ppermute | solution.py:26
  266.2 1.2 copy-start.7
  267.5 2.5 copy-start.2
  267.5 2.9 %copy-start.8 = (f32[1024,512]{1,0:T(8,128)S(1)}, f32[1024,512]{1,0:T(8,128)}, u32[]{:S(2)}) copy-start(f32[1024,512]{1,0:T(8,128)} %param.5) | copy-start | bytes 6291460
Sparse Core Ops, SparseCore 0:
  25.8 53.9 all-gather.1
